TPU v7x, 32 devices: a whole 2x2x4 slice. The times are simulated.
32 devices in a mesh: groups: 2 (over y), enc: 4 (over z), mp: 4 (over x, core).
Axes of the slice: x: 2, y: 2, z: 4, core: 2. Of those that a mesh axis runs over, the one named last changes fastest.
Arguments:
- hidden: bfloat16 [131072, 1024], P(('groups', 'enc'), 'mp'), parts along dimension 0, may hold values from -6 to 6
- proj_w: bfloat16 [1024, 128], P('mp'), may hold values from -0.1875 to 0.1875
- queries: bfloat16 [256, 32, 128], P(('groups', 'enc', 'mp')), parts along dimension 0, may hold values from -208 to 208
- lengths: int32 [512], P('groups'), parts along dimension 0, may hold values from 193 to 256, as said below
- candidates: int32 [256, 16], P(('groups', 'enc', 'mp')), parts along dimension 0, may hold values from 0 to 1023, as said below
Outputs:
- losses: float32 [256], P(('groups', 'enc', 'mp')), parts along dimension 0
- grad_w: float32 [2048, 128], P(('groups', 'mp')), parts along dimension 0
There are 2 independent parts, one for each index of `groups`. A program takes and returns all parts, laid end to end along the dimension named above; an argument that names none is the same for every part. Nothing has to cross between parts.
Inputs may be any that keep to these rules, and one draw needn't show every extreme that they name: Entries are global block numbers of this part. Of the candidates of the 8 queries of one device (aligned rows), at most 16 lie in the 64 blocks of any one device along enc+mp, where device k holds blocks k * 64 to (k + 1) * 64 - 1; some device receives exactly 16 from every device. Blocks may repeat. `lengths`: some passage has 256 tokens and some has 193.
All inputs are finite; a program needn't handle non-finite values.
Results may differ from a plain program's by a relative error of at most 0.0013.
The roundings to bfloat16 on the way count: a program that leaves them out, or rounds other values in their place, can miss the bound.
Values may be sent and summed in bfloat16 or wider, within the bound.
No kernel may reach another device: no remote copies, remote signals or barrier semaphores. Data moves between devices by JAX's collectives and lax.ppermute only.
A program may use at most 128 MiB of HBM per device.

v0:
```python
import jax
import jax.numpy as jnp
from jax import lax
from jax.sharding import PartitionSpec as P

L = 256
BLK = 64


def block_valid(block_ids, lengths):
    per_passage = L // BLK
    passage = block_ids // per_passage
    within = block_ids % per_passage
    positions = within[..., None] * BLK + jnp.arange(BLK, dtype=jnp.int32)
    return positions < lengths[passage][..., None]


def soft_max_sim(sim_tile, valid_mask):
    masked = jnp.where(valid_mask, sim_tile, jnp.float32(-1e30))
    peak = jnp.max(masked, -1, keepdims=True)
    shifted = jnp.exp(masked - peak)
    running = jnp.sum(shifted, -1, keepdims=True)
    scores = jnp.mean(peak[..., 0] + jnp.log(running[..., 0]), -1)
    weights = (shifted / running).astype(jnp.bfloat16)
    return (scores, weights)


def loss_terms(scores):
    margins = scores[:, 1:] - scores[:, :1]
    losses = jnp.mean(jax.nn.softplus(margins), 1)
    slopes = jax.nn.sigmoid(margins) / (scores.shape[1] - 1)
    d_score = jnp.concatenate([-jnp.sum(slopes, 1, keepdims=True), slopes], 1)
    return (losses, d_score)


def left_product(left, right):
    return lax.dot_general(
        left, right, (((0,), (0,)), ((), ())), preferred_element_type=jnp.float32
    )


def local(hidden, proj_w, queries, lengths, candidates):
    mp_count = lax.axis_size("mp")
    owners = lax.axis_size("enc") * mp_count
    row_share = hidden.shape[0] // mp_count
    emb_width = proj_w.shape[1]
    qry_dev = queries.shape[0]
    query_len = queries.shape[1]
    cand_count = candidates.shape[1]
    blk_dev = row_share // BLK
    slot_count = qry_dev * cand_count
    capacity = 2 * slot_count // owners
    e_pre = lax.psum_scatter(
        jnp.dot(hidden, proj_w, preferred_element_type=jnp.float32),
        "mp",
        scatter_dimension=0,
        tiled=True,
    )
    scale = lax.rsqrt(jnp.sum(e_pre * e_pre, -1, keepdims=True) + 1e-06)
    embedded = (e_pre * scale).astype(jnp.bfloat16)
    local_blocks = embedded.reshape(blk_dev, BLK, emb_width)
    flat_cand = candidates.reshape(-1)
    owner_of = flat_cand // blk_dev
    slot_ids = jnp.arange(slot_count, dtype=jnp.int32)
    same_owner = owner_of[:, None] == owner_of[None, :]
    earlier = slot_ids[None, :] < slot_ids[:, None]
    rank_in = jnp.sum(jnp.where(same_owner & earlier, 1, 0), 1).astype(jnp.int32)
    dest = owner_of * capacity + rank_in
    wanted = jnp.zeros((owners * capacity,), jnp.int32).at[dest].set(flat_cand % blk_dev)
    served = lax.all_to_all(
        wanted.reshape(owners, capacity), ("enc", "mp"), split_axis=0, concat_axis=0, tiled=True
    ).reshape(-1)
    grad_emb = jnp.zeros((blk_dev, BLK, emb_width), jnp.float32)
    tiles = local_blocks[served].reshape(owners, capacity, BLK, emb_width)
    arrived = lax.all_to_all(tiles, ("enc", "mp"), split_axis=0, concat_axis=0, tiled=True).reshape(
        owners * capacity, BLK, emb_width
    )
    mine = arrived[dest].reshape(qry_dev, cand_count, BLK, emb_width)
    valid_mask = block_valid(candidates, lengths)
    sim_tile = jnp.einsum("qie,qcje->qcij", queries, mine, preferred_element_type=jnp.float32)
    scores, weights = soft_max_sim(sim_tile, valid_mask[:, :, None, :])
    losses, d_score = loss_terms(scores)
    occ_grad = jnp.einsum("qcij,qie->qcje", weights, queries, preferred_element_type=jnp.float32)
    occ_grad = (occ_grad * (d_score / query_len)[:, :, None, None]).astype(jnp.bfloat16)
    outgoing = jnp.zeros((owners * capacity, BLK, emb_width), jnp.bfloat16)
    outgoing = outgoing.at[dest].set(occ_grad.reshape(slot_count, BLK, emb_width))
    returned = lax.all_to_all(
        outgoing.reshape(owners, capacity, BLK, emb_width),
        ("enc", "mp"),
        split_axis=0,
        concat_axis=0,
        tiled=True,
    )
    grad_emb = grad_emb.at[served].add(returned.reshape(-1, BLK, emb_width).astype(jnp.float32))
    grad_flat = grad_emb.reshape(row_share, emb_width)
    dot_e = jnp.sum(e_pre * grad_flat, -1, keepdims=True)
    de_pre = (scale * grad_flat - e_pre * (scale * scale * scale) * dot_e).astype(jnp.bfloat16)
    partial_w = left_product(hidden, lax.all_gather(de_pre, "mp", axis=0, tiled=True))
    grad_w = lax.psum(partial_w, "enc")
    return (losses, grad_w)


def solution(mesh):
    return jax.shard_map(
        local,
        mesh=mesh,
        in_specs=(
            P(("groups", "enc"), "mp"),
            P("mp", None),
            P(("groups", "enc", "mp"), None, None),
            P("groups"),
            P(("groups", "enc", "mp"), None),
        ),
        out_specs=(P(("groups", "enc", "mp")), P(("groups", "mp"), None)),
        check_vma=False,
    )
```

profile of v0, /device:TPU:0, one launch (start us, length us, event | category | flops | bytes accessed | tf_op | source)
XLA Modules:
  0.0 446.6 jit_solution(9475051947328319691)
XLA Ops:
  8.0 8.9 %fusion.22 = f32[16384,128]{1,0:T(8,128)} fusion(bf16[16384,256]{1,0:T(8,128)(2,1)} %param.5, bf16[256,128]{1,0:T(8,128)(2,1)S(1)} %copy-done), kind=kOutput, calls=%fused_computation.74 | convolution fusion | flops 1073741824 | bytes 16842752 | tf_op jit(solution)/shard_map/dot_general | solution.py:54
  18.0 1.0 scatter_custom_fusion
  19.1 13.6 %all_to_all.19 = s32[16,1,16]{2,1,0:T(1,128)S(1)} all-to-all(s32[16,1,16]{2,1,0:T(1,128)S(1)} %all_to_all.12), channel_id=1, replica_groups=mesh['groups'=2,'enc'=4,'mp'=4] {'enc','mp'}, dimensions={0} | all-to-all | bytes 2048 | tf_op jit(solution)/shard_map/all_to_all | solution.py:70
  33.9 57.6 %reduce-scatter.2.cloned.1.call-done = f32[4096,128]{1,0:T(8,128)} async-done(((f32[16384,128]{1,0:T(8,128)}), f32[4096,128]{1,0:T(8,128)}) %reduce-scatter.2.cloned.1.call-update) | async-done | bytes 2097168 | tf_op jit(solution)/shard_map/reduce_scatter | solution.py:53
  91.5 2.4 multiply_reduce_fusion
  94.6 3.1 gather_fusion.1
  97.7 4.8 %all-to-all-start.1 = ((bf16[16,16,64,128]{3,2,1,0:T(8,128)(2,1)}), bf16[16,16,64,128]{3,2,1,0:T(8,128)(2,1)}, u32[]{:S(2)}, u32[]{:S(2)}) async-start(bf16[16,16,64,128]{3,2,1,0:T(8,128)(2,1)} %bitcast.55), calls=%async_computation.2 | async-start | bytes 8388608 | tf_op jit(solution)/shard_map/all_to_all | solution.py:75
  103.2 1.3 gather_fusion
  104.7 75.5 %all-to-all-done.1 = bf16[16,16,64,128]{3,2,1,0:T(8,128)(2,1)} async-done(((bf16[16,16,64,128]{3,2,1,0:T(8,128)(2,1)}), bf16[16,16,64,128]{3,2,1,0:T(8,128)(2,1)}, u32[]{:S(2)}, u32[]{:S(2)}) %all-to-all-start.1) | async-done | bytes 4194336 | tf_op jit(solution)/shard_map/all_to_all | solution.py:75
  180.2 4.4 gather_fusion.2
  184.5 3.8 bitcast_reduce_fusion
  188.3 1.3 fusion.4
  190.3 4.4 multiply_convert_fusion
  194.7 3.0 broadcast_in_dim.32
  197.7 15.7 %scatter_fusion = bf16[256,64,128]{2,1,0:T(8,128)(2,1)} fusion(bf16[256,64,128]{2,1,0:T(8,128)(2,1)} %broadcast_in_dim.32, s32[128]{0:T(128)S(1)} %fusion.17, bf16[128,64,128]{2,1,0:T(8,128)(2,1)S(1)} %bitcast.57), kind=kCustom, calls=%fused_computation.4 | custom fusion | bytes 6291968 | tf_op jit(solution)/shard_map/scatter | solution.py:86
  213.4 111.9 %all_to_all.20 = bf16[16,16,64,128]{3,2,1,0:T(8,128)(2,1)S(1)} all-to-all(bf16[16,16,64,128]{3,2,1,0:T(8,128)(2,1)} %bitcast.53), channel_id=1, replica_groups=mesh['groups'=2,'enc'=4,'mp'=4] {'enc','mp'}, dimensions={0} | all-to-all | bytes 8388608 | tf_op jit(solution)/shard_map/all_to_all | solution.py:87
  325.3 4.5 %bitcast_convert_fusion = f32[256,64,128]{2,1,0:T(8,128)} fusion(bf16[16,16,64,128]{3,2,1,0:T(8,128)(2,1)S(1)} %all_to_all.20), kind=kLoop, calls=%fused_computation.6 | loop fusion | flops 2097152 | bytes 12582912 | tf_op jit(solution)/shard_map/convert_element_type | solution.py:94
  330.1 26.3 %scatter_fusion.1 = f32[64,64,128]{2,1,0:T(8,128)S(1)} fusion(f32[64,64,128]{2,1,0:T(8,128)S(1)} %broadcast_in_dim.31, s32[256]{0:T(256)S(1)} %bitcast.59, f32[256,64,128]{2,1,0:T(8,128)} %bitcast_convert_fusion), kind=kCustom, calls=%fused_computation.5 | custom fusion | flops 2097152 | bytes 25166848 | tf_op jit(solution)/shard_map/scatter-add | solution.py:94
  356.3 2.4 fusion.2
  358.7 3.0 fusion.1
  361.8 35.2 %all-gather.2.cloned.1.call-done = bf16[16384,128]{1,0:T(8,128)(2,1)} async-done(((bf16[4096,128]{1,0:T(8,128)(2,1)}), bf16[16384,128]{1,0:T(8,128)(2,1)}) %all-gather.2.cloned.1.call-update) | async-done | bytes 4194320 | tf_op jit(solution)/shard_map/all_gather | solution.py:98
  397.0 6.8 %convolution_bitcast_fusion = f32[256,128]{0,1:T(8,128)} fusion(bf16[16384,128]{1,0:T(8,128)(2,1)} %all-gather.2.cloned.1.call-done, bf16[16384,256]{1,0:T(8,128)(2,1)} %param.5), kind=kOutput, calls=%fused_computation.20 | convolution fusion | flops 1073741824 | bytes 12713984 | tf_op jit(solution)/shard_map/dot_general | solution.py:37
  404.3 34.1 %all-reduce.2.cloned.1.call-done = f32[256,128]{0,1:T(8,128)} async-done(((f32[256,128]{0,1:T(8,128)}), f32[256,128]{0,1:T(8,128)}) %all-reduce.2.cloned.1.call-update) | async-done | bytes 131088 | tf_op jit(solution)/shard_map/psum | solution.py:99
  438.4 1.7 copy.16
  (48 shorter events, 6.3 us)
Async XLA Ops:
  7.2 0.8 copy-start
  7.2 84.4 %reduce-scatter.2.cloned.1.call-start = ((), (), s32[]{:S(2)}) async-start(), calls=%async_computation.4 | async-start | bytes 10485760 | tf_op jit(solution)/shard_map/reduce_scatter | solution.py:53
  16.9 0.7 copy-start.6
  91.5 2.4 copy-start.2
  97.7 82.5 %all-to-all-start.1 = ((bf16[16,16,64,128]{3,2,1,0:T(8,128)(2,1)}), bf16[16,16,64,128]{3,2,1,0:T(8,128)(2,1)}, u32[]{:S(2)}, u32[]{:S(2)}) async-start(bf16[16,16,64,128]{3,2,1,0:T(8,128)(2,1)} %bitcast.55), calls=%async_computation.2 | async-start | bytes 8388608 | tf_op jit(solution)/shard_map/all_to_all | solution.py:75
  102.5 0.7 copy-start.1
  102.5 294.4 %all-gather.2.cloned.1.call-start = ((), (), s32[]{:S(2)}) async-start(), calls=%async_computation.5 | async-start | bytes 5242880 | tf_op jit(solution)/shard_map/all_gather | solution.py:98
  180.2 4.4 copy-start.5
  194.7 3.0 copy-start.4
  356.3 2.4 copy-start.3
  361.7 76.7 %all-reduce.2.cloned.1.call-start = ((), (), s32[]{:S(2)}) async-start(), calls=%async_computation.6 | async-start | bytes 262144 | tf_op jit(solution)/shard_map/psum | solution.py:99
Sparse Core Ops, SparseCore 0:
  17.1 74.3 reduce-scatter.1
  361.8 35.0 all-gather.1
  403.9 34.4 all-reduce.1
where the time goes:
time: 448 us; the launch traced here: 447 us
  waiting for transfers between devices  202 us (45%)
  blocking collectives  125 us (28%)
  other arithmetic  42.4 us (9%)
  local copies, waits for them, and re-layouts  33.4 us (7%)
  matrix products  24 us (5%)
  between operations  14 us (3%)
  starting transfers between devices  4.9 us (1%)
    all_to_all x1, blocking collectives, local(): lax.all_to_all(outgoing.reshape(owners, capacity, BLK, emb_width), ('enc'...  112 us
    all_to_all x1, waiting for transfers between devices, local(): lax.all_to_all(tiles, ('enc', 'mp'), split_axis=0, concat_axis=0, tiled=T...  75.5 us
    reduce_scatter x1, waiting for transfers between devices, local(): lax.psum_scatter(jnp.dot(hidden, proj_w, preferred_element_type=jnp.float...  57.6 us
    all_gather x1, waiting for transfers between devices, local(): lax.all_gather(de_pre, 'mp', axis=0, tiled=True)  35.2 us
    psum x1, waiting for transfers between devices, local(): grad_w = lax.psum(partial_w, 'enc')  34.1 us
    scatter-add x1, other arithmetic, local(): grad_emb.at[served]  26.3 us
    scatter x1, local copies, waits for them, and re-layouts, local(): outgoing.at[dest].set(occ_grad.reshape(slot_count, BLK, emb_width))  15.7 us
    all_to_all x1, blocking collectives, local(): lax.all_to_all(wanted.reshape(owners, capacity), ('enc', 'mp'), split_axi...  13.6 us
  transfers between devices with their start and end apart: 4, of which 4 were waited for; matrix products, arithmetic and copies ran while one was open for 1% of the time, Pallas kernels for 0%

commit v1 on v0

--- a/solution.py
+++ b/solution.py
@@ -96,7 +96,7 @@
     dot_e = jnp.sum(e_pre * grad_flat, -1, keepdims=True)
     de_pre = (scale * grad_flat - e_pre * (scale * scale * scale) * dot_e).astype(jnp.bfloat16)
     partial_w = left_product(hidden, lax.all_gather(de_pre, "mp", axis=0, tiled=True))
-    grad_w = lax.psum(partial_w, "enc")
+    grad_w = jnp.sum(lax.all_gather(partial_w, "enc"), axis=0)
     return (losses, grad_w)
 
 

time: 448 us -> 429 us (0.958)
  waiting for transfers between devices: 202 us -> 168 us
  blocking collectives: 125 us -> 142 us
    psum x1 -> x0, waiting for transfers between devices: 34.1 us -> none  [local(): grad_w = lax.psum(partial_w, 'enc')]
    all_gather x0 -> x1, blocking collectives: none -> 16.1 us  [local(): grad_w = jnp.sum(lax.all_gather(partial_w, 'enc'), axis=0)]
  transfers between devices with their start and end apart: 4 -> 3, of which waited for: 4 -> 3; matrix products, arithmetic and copies ran while one was open for 1% -> 1% of each run, Pallas kernels for 0% -> 0%
where the time goes in v1:
time: 429 us; the launch traced here: 427 us
  waiting for transfers between devices  168 us (39%)
  blocking collectives  142 us (33%)
  other arithmetic  42.7 us (10%)
  local copies, waits for them, and re-layouts  32.8 us (8%)
  matrix products  23.3 us (5%)
  between operations  14.3 us (3%)
  starting transfers between devices  4.86 us (1%)
    all_to_all x1, blocking collectives, local(): lax.all_to_all(outgoing.reshape(owners, capacity, BLK, emb_width), ('enc'...  112 us
    all_to_all x1, waiting for transfers between devices, local(): lax.all_to_all(tiles, ('enc', 'mp'), split_axis=0, concat_axis=0, tiled=T...  75.5 us
    reduce_scatter x1, waiting for transfers between devices, local(): lax.psum_scatter(jnp.dot(hidden, proj_w, preferred_element_type=jnp.float...  57.6 us
    all_gather x1, waiting for transfers between devices, local(): lax.all_gather(de_pre, 'mp', axis=0, tiled=True)  34.7 us
    scatter-add x1, other arithmetic, local(): grad_emb.at[served]  26.3 us
    all_gather x1, blocking collectives, local(): grad_w = jnp.sum(lax.all_gather(partial_w, 'enc'), axis=0)  16.1 us
    scatter x1, local copies, waits for them, and re-layouts, local(): outgoing.at[dest].set(occ_grad.reshape(slot_count, BLK, emb_width))  15.7 us
    all_to_all x1, blocking collectives, local(): lax.all_to_all(wanted.reshape(owners, capacity), ('enc', 'mp'), split_axi...  13.6 us
  transfers between devices with their start and end apart: 3, of which 3 were waited for; matrix products, arithmetic and copies ran while one was open for 1% of the time, Pallas kernels for 0%

profile of v1, /device:TPU:0, one launch (start us, length us, event | category | flops | bytes accessed | tf_op | source)
XLA Modules:
  0.0 427.4 jit_solution(86447867838901148)
XLA Ops:
  7.2 0.8 copy-done
  8.0 8.9 %fusion.22 = f32[16384,128]{1,0:T(8,128)} fusion(bf16[16384,256]{1,0:T(8,128)(2,1)} %param.5, bf16[256,128]{1,0:T(8,128)(2,1)S(1)} %copy-done), kind=kOutput, calls=%fused_computation.74 | convolution fusion | flops 1073741824 | bytes 16842752 | tf_op jit(solution)/shard_map/dot_general | solution.py:54
  18.0 1.0 scatter_custom_fusion
  19.1 13.6 %all_to_all.19 = s32[16,1,16]{2,1,0:T(1,128)S(1)} all-to-all(s32[16,1,16]{2,1,0:T(1,128)S(1)} %all_to_all.12), channel_id=1, replica_groups=mesh['groups'=2,'enc'=4,'mp'=4] {'enc','mp'}, dimensions={0} | all-to-all | bytes 2048 | tf_op jit(solution)/shard_map/all_to_all | solution.py:70
  33.9 57.6 %reduce-scatter.2.cloned.1.call-done = f32[4096,128]{1,0:T(8,128)} async-done(((f32[16384,128]{1,0:T(8,128)}), f32[4096,128]{1,0:T(8,128)}) %reduce-scatter.2.cloned.1.call-update) | async-done | bytes 2097168 | tf_op jit(solution)/shard_map/reduce_scatter | solution.py:53
  91.5 2.4 multiply_reduce_fusion
  94.6 3.1 gather_fusion.1
  97.7 4.8 %all-to-all-start.1 = ((bf16[16,16,64,128]{3,2,1,0:T(8,128)(2,1)}), bf16[16,16,64,128]{3,2,1,0:T(8,128)(2,1)}, u32[]{:S(2)}, u32[]{:S(2)}) async-start(bf16[16,16,64,128]{3,2,1,0:T(8,128)(2,1)} %bitcast.57), calls=%async_computation.2 | async-start | bytes 8388608 | tf_op jit(solution)/shard_map/all_to_all | solution.py:75
  103.2 1.3 gather_fusion
  104.7 75.5 %all-to-all-done.1 = bf16[16,16,64,128]{3,2,1,0:T(8,128)(2,1)} async-done(((bf16[16,16,64,128]{3,2,1,0:T(8,128)(2,1)}), bf16[16,16,64,128]{3,2,1,0:T(8,128)(2,1)}, u32[]{:S(2)}, u32[]{:S(2)}) %all-to-all-start.1) | async-done | bytes 4194336 | tf_op jit(solution)/shard_map/all_to_all | solution.py:75
  180.2 4.4 %gather_fusion.2 = bf16[128,64,128]{2,1,0:T(8,128)(2,1)} fusion(bf16[256,64,128]{2,1,0:T(8,128)(2,1)} %bitcast.5, s32[1024]{0:T(1024)S(1)} %pad_clamp_fusion), kind=kCustom, calls=%fused_computation.2 | custom fusion | bytes 4194816 | tf_op jit(solution)/shard_map/gather | solution.py:78
  184.5 3.8 bitcast_reduce_fusion
  188.3 1.3 fusion.4
  190.3 4.4 %multiply_convert_fusion = bf16[8,16,64,128]{3,2,1,0:T(8,128)(2,1)} fusion(f32[8,16]{1,0:T(8,128)S(1)} %maximum_multiply_fusion, f32[8,16,64,32]{2,3,1,0:T(8,128)S(1)} %get-tuple-element.18, f32[8,16,32]{2,1,0:T(8,128)S(1)} %fusion.4, f32[8,16,32]{2,1,0:T(8,128)S(1)} %get-tuple-element.17, pred[8,16,64]{2,1,0:T(8,128)(4,1)S(1)} %add_compare_fusion, ...), kind=kOutput, calls=%fused_computation.7 | convolution fusion | flops 70254592 | bytes 3252736 | tf_op jit(solution)/shard_map/qcij,qie->qcje/dot_general | solution.py:83
  194.7 3.0 broadcast_in_dim.32
  197.7 15.7 %scatter_fusion = bf16[256,64,128]{2,1,0:T(8,128)(2,1)} fusion(bf16[256,64,128]{2,1,0:T(8,128)(2,1)} %broadcast_in_dim.32, s32[128]{0:T(128)S(1)} %fusion.17, bf16[128,64,128]{2,1,0:T(8,128)(2,1)S(1)} %bitcast.59), kind=kCustom, calls=%fused_computation.4 | custom fusion | bytes 6291968 | tf_op jit(solution)/shard_map/scatter | solution.py:86
  213.4 111.9 %all_to_all.20 = bf16[16,16,64,128]{3,2,1,0:T(8,128)(2,1)S(1)} all-to-all(bf16[16,16,64,128]{3,2,1,0:T(8,128)(2,1)} %bitcast.55), channel_id=1, replica_groups=mesh['groups'=2,'enc'=4,'mp'=4] {'enc','mp'}, dimensions={0} | all-to-all | bytes 8388608 | tf_op jit(solution)/shard_map/all_to_all | solution.py:87
  325.3 4.5 %bitcast_convert_fusion = f32[256,64,128]{2,1,0:T(8,128)} fusion(bf16[16,16,64,128]{3,2,1,0:T(8,128)(2,1)S(1)} %all_to_all.20), kind=kLoop, calls=%fused_computation.6 | loop fusion | flops 2097152 | bytes 12582912 | tf_op jit(solution)/shard_map/convert_element_type | solution.py:94
  330.1 26.3 %scatter_fusion.1 = f32[64,64,128]{2,1,0:T(8,128)S(1)} fusion(f32[64,64,128]{2,1,0:T(8,128)S(1)} %broadcast_in_dim.31, s32[256]{0:T(256)S(1)} %bitcast.61, f32[256,64,128]{2,1,0:T(8,128)} %bitcast_convert_fusion), kind=kCustom, calls=%fused_computation.5 | custom fusion | flops 2097152 | bytes 25166848 | tf_op jit(solution)/shard_map/scatter-add | solution.py:94
  356.3 2.4 fusion.2
  358.7 3.0 fusion.1
  362.2 34.7 %all-gather.3.cloned.1.call-done = bf16[16384,128]{1,0:T(8,128)(2,1)} async-done(((bf16[4096,128]{1,0:T(8,128)(2,1)}), bf16[16384,128]{1,0:T(8,128)(2,1)}) %all-gather.3.cloned.1.call-update) | async-done | bytes 4194320 | tf_op jit(solution)/shard_map/all_gather | solution.py:98
  397.0 6.2 %convolution_bitcast_fusion = f32[256,128]{0,1:T(8,128)S(1)} fusion(bf16[16384,128]{1,0:T(8,128)(2,1)} %all-gather.3.cloned.1.call-done, bf16[16384,256]{1,0:T(8,128)(2,1)} %param.5), kind=kOutput, calls=%fused_computation.20 | convolution fusion | flops 1073741824 | bytes 12713984 | tf_op jit(solution)/shard_map/dot_general | solution.py:37
  403.1 16.1 %all-gather = f32[1024,128]{0,1:T(8,128)S(1)} all-gather(f32[256,128]{0,1:T(8,128)S(1)} %convolution_bitcast_fusion), channel_id=2, replica_groups=mesh['groups'=2,'enc'=4,'mp'=4] {'enc'}, dimensions={0}, use_global_device_ids=true | all-gather | bytes 655360 | tf_op jit(solution)/shard_map/all_gather | solution.py:99
  (48 shorter events, 6.7 us)
Async XLA Ops:
  7.2 0.8 copy-start
  7.2 84.4 %reduce-scatter.2.cloned.1.call-start = ((), (), s32[]{:S(2)}) async-start(), calls=%async_computation.4 | async-start | bytes 10485760 | tf_op jit(solution)/shard_map/reduce_scatter | solution.py:53
  16.9 0.7 copy-start.6
  91.5 2.4 copy-start.2
  97.7 82.5 %all-to-all-start.1 = ((bf16[16,16,64,128]{3,2,1,0:T(8,128)(2,1)}), bf16[16,16,64,128]{3,2,1,0:T(8,128)(2,1)}, u32[]{:S(2)}, u32[]{:S(2)}) async-start(bf16[16,16,64,128]{3,2,1,0:T(8,128)(2,1)} %bitcast.57), calls=%async_computation.2 | async-start | bytes 8388608 | tf_op jit(solution)/shard_map/all_to_all | solution.py:75
  102.5 0.7 copy-start.1
  102.5 294.4 %all-gather.3.cloned.1.call-start = ((), (), s32[]{:S(2)}) async-start(), calls=%async_computation.5 | async-start | bytes 5242880 | tf_op jit(solution)/shard_map/all_gather | solution.py:98
  180.2 4.4 %copy-start.5 = (bf16[8,32,128]{2,1,0:T(8,128)(2,1)S(1)}, bf16[8,32,128]{2,1,0:T(8,128)(2,1)}, u32[]{:S(2)}) copy-start(bf16[8,32,128]{2,1,0:T(8,128)(2,1)} %param.7) | copy-start | bytes 196612
  194.7 3.0 copy-start.4
  356.3 2.4 copy-start.3
Sparse Core Ops, SparseCore 0:
  17.1 74.3 reduce-scatter.1
  361.8 35.0 all-gather.2
